TPU v7x, 128 devices: a whole 4x4x4 slice. The times are simulated.
128 devices in a mesh: prow: 8 (over x, core), pcol: 16 (over y, z).
Axes of the slice: x: 4, y: 4, z: 4, core: 2. Of those that a mesh axis runs over, the one named last changes fastest.
Arguments:
- basis: bfloat16 [512, 256], replicated, may hold values from -0.25 to 0.25
- potentials: float32 [8, 512], replicated, may hold values from -6 to 6
- orbitals: bfloat16 [64, 512], P('pcol'), may hold values from -6 to 6
- chan_orbital: int32 [256], replicated, may hold values from 0 to 63
- pair_list: int32 [24576, 3], P(('prow', 'pcol')), may hold values from 0 to 255, as said below
- slot_list: int32 [24576], P(('prow', 'pcol')), may hold values from 0 to 255
- coefs: float32 [24576, 2], P(('prow', 'pcol')), may hold values from -6 to 6
- exchange_ops: bfloat16 [24576, 128, 256], P(('prow', 'pcol')), may hold values from -1.1953125 to 1.1953125
Outputs:
- hamiltonian: bfloat16 [32, 8, 2, 16, 256, 256], P(None, 'prow', None, 'pcol')
Inputs may be any that keep to these rules, and one draw needn't show every extreme that they name: `pair_list`: columns 0 and 1 are channels a, b; column 2 is a multipole order below 8. (b // 16 - a // 16) modulo 256 // 16 is below 2. Terms of one device with the same slot s have the same two channels, and the block (a, b) belongs to owner s // 2 in prow-major order: a % 8 and b % 16 are that owner's prow and pcol indices.
All inputs are finite; a program needn't handle non-finite values.
Results may differ from a plain program's by a relative error of at most 0.0058.
Values may be sent and summed in bfloat16 or wider, within the bound.
No kernel may reach another device: no remote copies, remote signals or barrier semaphores. Data moves between devices by JAX's collectives and lax.ppermute only.
A program may use at most 320 MiB of HBM per device.

v0:
```python
import jax
import jax.numpy as jnp
from jax import lax
from jax.sharding import PartitionSpec as P

CAP = 2
BAND = 2
RBLK = 32


def split_bf16(values):
    high = values.astype(jnp.bfloat16)
    low = (values - high.astype(jnp.float32)).astype(jnp.bfloat16)
    return (high, low)


def on_device(basis, potentials, orbitals, chan_orbital, pair_list, slot_list, coefs, exchange_ops):
    all_orbitals = lax.all_gather(orbitals, "pcol", axis=0, tiled=True)
    row_devs = lax.axis_size("prow")
    col_devs = lax.axis_size("pcol")
    slot_count = row_devs * col_devs * CAP
    chan_count = chan_orbital.shape[0]
    orb_count = all_orbitals.shape[0]
    point_count = basis.shape[0]
    spline_count = basis.shape[1]
    inner_count = exchange_ops.shape[1]
    term_count = exchange_ops.shape[0]
    col_groups = chan_count // col_devs
    block_count = RBLK * BAND
    first_chan = pair_list[:, 0]
    second_chan = pair_list[:, 1]
    multipole = pair_list[:, 2]
    channels = jnp.arange(chan_count, dtype=jnp.int32)
    orb_ids = jnp.arange(orb_count, dtype=jnp.int32)
    first_orb = jnp.sum(
        jnp.where(first_chan[:, None] == channels[None, :], chan_orbital[None, :], 0), axis=1
    )
    second_orb = jnp.sum(
        jnp.where(second_chan[:, None] == channels[None, :], chan_orbital[None, :], 0), axis=1
    )
    first_rows = jnp.dot(
        (first_orb[:, None] == orb_ids[None, :]).astype(jnp.bfloat16),
        all_orbitals,
        preferred_element_type=jnp.float32,
    )
    second_rows = jnp.dot(
        (second_orb[:, None] == orb_ids[None, :]).astype(jnp.bfloat16),
        all_orbitals,
        preferred_element_type=jnp.float32,
    )
    pick_pot = (
        multipole[:, None] == jnp.arange(potentials.shape[0], dtype=jnp.int32)[None, :]
    ).astype(jnp.float32)
    pot_rows = jnp.dot(pick_pot, potentials, precision=lax.Precision.HIGHEST)
    radial = coefs[:, 0:1] * pot_rows + coefs[:, 1:2] * (first_rows * second_rows)
    matches = slot_list[None, :] == jnp.arange(slot_count, dtype=jnp.int32)[:, None]
    slot_weight = jnp.dot(
        matches.astype(jnp.float32), radial, precision=lax.Precision.HIGHEST
    ).astype(jnp.bfloat16)
    exchange_rows = exchange_ops.reshape(term_count, inner_count * spline_count)
    slot_exchange = jnp.dot(
        matches.astype(jnp.bfloat16), exchange_rows, preferred_element_type=jnp.float32
    ).astype(jnp.bfloat16)
    offset = jnp.mod(second_chan // col_devs - first_chan // col_devs, col_groups)
    block_index = first_chan // row_devs * BAND + offset
    slot_ids = jnp.max(jnp.where(matches, block_index[None, :], -1), axis=1)
    payload = inner_count * spline_count + point_count + 1
    width = -(-payload // 128) * 128
    packed = jnp.concatenate(
        [
            slot_exchange,
            slot_weight,
            slot_ids.astype(jnp.bfloat16)[:, None],
            jnp.zeros((slot_count, width - payload), jnp.bfloat16),
        ],
        axis=1,
    )
    received = lax.all_to_all(packed, ("prow", "pcol"), 0, 0, tiled=True)
    idents = received[:, payload - 1].astype(jnp.float32).astype(jnp.int32)
    select = (jnp.arange(block_count, dtype=jnp.int32)[:, None] == idents[None, :]).astype(
        jnp.bfloat16
    )
    summed = jnp.dot(select, received[:, : payload - 1], preferred_element_type=jnp.float32)
    exchange_sum = summed[:, : inner_count * spline_count].reshape(
        block_count, inner_count, spline_count
    )
    weight_sum = summed[:, inner_count * spline_count :]
    basis_float = basis.astype(jnp.float32)
    scaled_high, scaled_low = split_bf16(weight_sum[:, :, None] * basis_float[None])
    exchange_high, exchange_low = split_bf16(exchange_sum)
    inner_rows = basis[:inner_count]
    tiles = (
        jnp.einsum("qa,gqb->gab", basis, scaled_high, preferred_element_type=jnp.float32)
        + jnp.einsum("qa,gqb->gab", basis, scaled_low, preferred_element_type=jnp.float32)
        + jnp.einsum("qa,gqb->gab", inner_rows, exchange_high, preferred_element_type=jnp.float32)
        + jnp.einsum("qa,gqb->gab", inner_rows, exchange_low, preferred_element_type=jnp.float32)
    )
    return tiles.astype(jnp.bfloat16).reshape(RBLK, 1, BAND, 1, spline_count, spline_count)


def solution(mesh):
    placed = (
        P(),
        P(),
        P("pcol", None),
        P(),
        P(("prow", "pcol"), None),
        P(("prow", "pcol")),
        P(("prow", "pcol"), None),
        P(("prow", "pcol"), None, None),
    )
    return jax.shard_map(
        on_device,
        mesh=mesh,
        in_specs=placed,
        out_specs=P(None, "prow", None, "pcol", None, None),
        check_vma=False,
    )
```

profile of v0, /device:TPU:23, one launch (start us, length us, event | category | flops | bytes accessed | tf_op | source)
XLA Modules:
  0.0 489.6 jit_solution(6347302952289938058)
XLA Ops:
  0.0 0.0 copy-start
  0.0 0.0 copy-start.4
  0.0 0.8 fusion.31
  0.8 0.8 fusion.30
  1.6 0.8 select_reduce_fusion
  2.4 0.9 select_reduce_fusion.1
  3.3 0.2 convert_element_type.87
  3.6 18.1 %all-gather = bf16[16,4,512]{2,1,0:T(4,128)(2,1)S(1)} all-gather(bf16[1,4,512]{2,1,0:T(4,128)(2,1)} %bitcast.40), channel_id=1, replica_groups=mesh['prow'=8,'pcol'=16] {'pcol'}, dimensions={0}, use_global_device_ids=true | all-gather | bytes 69632 | tf_op jit(solution)/shard_map/all_gather | solution.py:18
  21.7 0.2 fusion.19
  22.0 0.3 fusion.14
  22.3 0.0 copy-done
  22.3 0.4 fusion.13
  22.6 1.2 convolution_convert_fusion.1
  23.8 0.1 concatenate.9
  23.9 13.9 %copy.34 = bf16[24,8,128,256]{3,1,2,0:T(8,128)(2,1)} copy(bf16[24,8,128,256]{3,2,1,0:T(8,128)(2,1)} %bitcast.32) | data formatting | bytes 25165824
  37.8 0.0 copy-done.4
  37.8 12.7 %convolution_convert_fusion = bf16[256,32768]{1,0:T(8,128)(2,1)} fusion(bf16[192,32768]{1,0:T(8,128)(2,1)} %bitcast.28, s32[192]{0:T(256)S(1)} %copy-done.4), kind=kOutput, calls=%fused_computation.2 | convolution fusion | flops 3229663232 | bytes 29360896 | tf_op jit(solution)/shard_map/dot_general | solution.py:61
  50.6 27.1 %concatenate.8 = bf16[128,2,32768]{2,1,0:T(2,128)(2,1)} reshape(bf16[256,32768]{1,0:T(8,128)(2,1)} %convolution_convert_fusion) | data formatting | bytes 33554432 | tf_op jit(solution)/shard_map/concatenate | solution.py:69
  77.6 14.1 %constant_dynamic-update-slice_fusion.1 = bf16[128,2,33408]{2,1,0:T(2,128)(2,1)} fusion(bf16[128,2,32768]{2,1,0:T(2,128)(2,1)} %concatenate.8), kind=kLoop, calls=%fused_computation.47 | loop fusion | bytes 33554432
  91.8 0.9 constant_dynamic-update-slice_fusion
  92.7 3.3 dynamic-update-slice.2
  96.0 21.9 %dynamic-update-slice.3 = bf16[128,2,33408]{2,1,0:T(2,128)(2,1)} dynamic-update-slice(bf16[128,2,33408]{2,1,0:T(2,128)(2,1)} %dynamic-update-slice.2, bf16[128,2,127]{2,1,0:T(2,128)(2,1)S(1)} %broadcast_in_dim.52, s32[]{} %constant.60, s32[]{} %constant.60, s32[]{} %constant.63) | dynamic-update-slice | bytes 130052 | tf_op jit(solution)/shard_map/concatenate | solution.py:69
  117.9 0.0 copy-start.3
  117.9 14.7 %all-to-all-start = ((bf16[128,2,33408]{2,1,0:T(2,128)(2,1)}), bf16[128,2,33408]{2,1,0:T(2,128)(2,1)}, u32[]{:S(2)}, u32[]{:S(2)}) async-start(bf16[128,2,33408]{2,1,0:T(2,128)(2,1)} %dynamic-update-slice.3), calls=%async_computation | async-start | bytes 34209792 | tf_op jit(solution)/shard_map/all_to_all | solution.py:78
  132.6 0.0 copy-done.3
  132.6 0.1 copy.30
  132.8 239.9 %all-to-all-done = bf16[128,2,33408]{2,1,0:T(2,128)(2,1)} async-done(((bf16[128,2,33408]{2,1,0:T(2,128)(2,1)}), bf16[128,2,33408]{2,1,0:T(2,128)(2,1)}, u32[]{:S(2)}, u32[]{:S(2)}) %all-to-all-start) | async-done | bytes 17104928 | tf_op jit(solution)/shard_map/all_to_all | solution.py:78
  372.7 25.3 %all_to_all.7 = bf16[256,33408]{1,0:T(8,128)(2,1)} reshape(bf16[128,2,33408]{2,1,0:T(2,128)(2,1)} %all-to-all-done) | data formatting | bytes 34209792 | tf_op jit(solution)/shard_map/all_to_all | solution.py:78
  398.1 1.0 convert_reduce_fusion
  399.0 7.5 %fusion.2 = f32[64,33280]{1,0:T(8,128)S(1)} fusion(bf16[256,33408]{1,0:T(8,128)(2,1)} %all_to_all.7, s32[256]{0:T(256)S(1)} %convert_reduce_fusion), kind=kOutput, calls=%fused_computation.5 | convolution fusion | flops 1090535424 | bytes 25560064 | tf_op jit(solution)/shard_map/dot_general | solution.py:83
  406.5 3.9 slice.43
  410.5 8.0 %fusion.4 = f32[64,256,256]{2,1,0:T(8,128)} fusion(f32[512,256]{0,1:T(8,128)S(1)} %copy.30, f32[64,512]{1,0:T(8,128)S(1)} %slice.42, bf16[512,256]{1,0:T(8,128)(2,1)S(1)} %copy-done.3), kind=kOutput, calls=%fused_computation.7 | convolution fusion | flops 4336910336 | bytes 17694720 | tf_op jit(solution)/shard_map/qa,gqb->gab/dot_general | solution.py:94
  418.5 0.0 copy-start.2
  418.5 8.0 %fusion.1 = f32[64,256,256]{2,1,0:T(8,128)} fusion(f32[512,256]{0,1:T(8,128)S(1)} %copy.30, f32[64,512]{1,0:T(8,128)S(1)} %slice.42, bf16[512,256]{1,0:T(8,128)(2,1)S(1)} %copy-done.3), kind=kOutput, calls=%fused_computation.4 | convolution fusion | flops 4311744512 | bytes 17694720 | tf_op jit(solution)/shard_map/qa,gqb->gab/dot_general | solution.py:93
  426.5 0.0 copy-done.2
  426.5 5.9 %copy.35 = f32[8,8,128,256]{3,2,1,0:T(8,128)} copy(f32[8,8,128,256]{3,1,2,0:T(8,128)S(1)} %bitcast.30) | data formatting | bytes 16777216
  432.4 9.0 %copy.31 = f32[64,128,256]{1,2,0:T(8,128)} copy(f32[64,128,256]{2,1,0:T(8,128)} %bitcast.31) | data formatting | bytes 16777216 | tf_op jit(solution)/shard_map/reshape | solution.py:84
  441.4 11.4 %fusion.11 = f32[64,256,256]{2,1,0:T(8,128)} fusion(f32[64,128,256]{1,2,0:T(8,128)} %copy.31, bf16[512,256]{1,0:T(8,128)(2,1)S(1)} %copy-done.3), kind=kOutput, calls=%fused_computation.15 | convolution fusion | flops 1075838976 | bytes 25231360 | tf_op jit(solution)/shard_map/qa,gqb->gab/dot_general | solution.py:95
  452.8 0.0 copy-start.1
  452.8 24.9 %add_convert_fusion = bf16[64,256,256]{2,1,0:T(8,128)(2,1)} fusion(f32[64,256,256]{2,1,0:T(8,128)} %fusion.11, f32[64,256,256]{2,1,0:T(8,128)} %fusion.1, f32[64,256,256]{2,1,0:T(8,128)} %fusion.4, f32[64,128,256]{1,2,0:T(8,128)} %copy.31, bf16[512,256]{1,0:T(8,128)(2,1)S(1)} %copy-done.3), kind=kOutput, calls=%fused_computation.8 | convolution fusion | flops 1098907648 | bytes 67174400 | tf_op jit(solution)/shard_map/qa,gqb->gab/dot_general | solution.py:96
  477.7 11.9 %copy.33 = bf16[32,1,2,1,256,256]{5,4,3,2,1,0:T(8,128)(2,1)} copy(bf16[32,1,2,1,256,256]{4,5,2,0,3,1:T(8,128)(2,1)} %bitcast.29) | data formatting | bytes 16777216 | tf_op jit(solution)/shard_map/reshape | solution.py:98
  489.6 0.0 copy-done.1
  (5 shorter events, 0.1 us)
Async XLA Ops:
  0.0 22.3 %copy-start = (f32[8,512]{1,0:T(8,128)S(1)}, f32[8,512]{1,0:T(8,128)}, u32[]{:S(2)}) copy-start(f32[8,512]{1,0:T(8,128)} %param.9) | copy-start | bytes 49156
  0.0 37.8 %copy-start.4 = (s32[192]{0:T(256)S(1)}, s32[192]{0:T(256)}, u32[]{:S(2)}) copy-start(s32[192]{0:T(256)} %param.13) | copy-start | bytes 2308
  117.9 14.8 %copy-start.3 = (bf16[512,256]{1,0:T(8,128)(2,1)S(1)}, bf16[512,256]{1,0:T(8,128)(2,1)}, u32[]{:S(2)}) copy-start(bf16[512,256]{1,0:T(8,128)(2,1)} %param.8) | copy-start | bytes 786436
  117.9 254.8 %all-to-all-start = ((bf16[128,2,33408]{2,1,0:T(2,128)(2,1)}), bf16[128,2,33408]{2,1,0:T(2,128)(2,1)}, u32[]{:S(2)}, u32[]{:S(2)}) async-start(bf16[128,2,33408]{2,1,0:T(2,128)(2,1)} %dynamic-update-slice.3), calls=%async_computation | async-start | bytes 34209792 | tf_op jit(solution)/shard_map/all_to_all | solution.py:78
  418.5 8.0 %copy-start.2 = (f32[64,32768]{1,0:T(8,128)S(1)}, f32[64,32768]{1,0:T(8,128)}, u32[]{:S(2)}) copy-start(f32[64,32768]{1,0:T(8,128)} %slice.43) | copy-start | bytes 25165828
  452.8 36.8 %copy-start.1 = (f32[8,512]{1,0:T(8,128)S(1)}, f32[8,512]{1,0:T(8,128)}, u32[]{:S(2)}) copy-start(f32[8,512]{1,0:T(8,128)} %param.9) | copy-start | bytes 49156
where the time goes:
time: 492 us; the launch traced here: 490 us
  waiting for transfers between devices  240 us (49%)
  local copies, waits for them, and re-layouts  139 us (28%)
  matrix products  74.7 us (15%)
  blocking collectives  18.1 us (4%)
  starting transfers between devices  14.7 us (3%)
    all_to_all x1, waiting for transfers between devices, on_device(): received = lax.all_to_all(packed, ('prow', 'pcol'), 0, 0, tiled=True)  240 us
    concatenate x3, local copies, waits for them, and re-layouts, on_device(): jnp.concatenate([slot_exchange, slot_weight, slot_ids.astype(jnp.bfloat16...  49.1 us
    unnamed x16, local copies, waits for them, and re-layouts  38.1 us
    all_to_all x1, local copies, waits for them, and re-layouts, on_device(): received = lax.all_to_all(packed, ('prow', 'pcol'), 0, 0, tiled=True)  25.3 us
    dot_general x1, matrix products, on_device(): jnp.einsum('qa,gqb->gab', inner_rows, exchange_low, preferred_element_typ...  24.9 us
    all_gather x1, blocking collectives, on_device(): all_orbitals = lax.all_gather(orbitals, 'pcol', axis=0, tiled=True)  18.1 us
    all_to_all x1, starting transfers between devices, on_device(): received = lax.all_to_all(packed, ('prow', 'pcol'), 0, 0, tiled=True)  14.7 us
    dot_general x1, matrix products, on_device(): jnp.dot(matches.astype(jnp.bfloat16), exchange_rows, preferred_element_ty...  12.7 us
  transfers between devices with their start and end apart: 1, of which 1 were waited for; matrix products, arithmetic and copies ran while one was open for 0% of the time, Pallas kernels for 0%

commit v1 on v0

--- a/solution.py
+++ b/solution.py
@@ -8,6 +8,19 @@
 RBLK = 32
 
 
+def collect(x, axis, dim):
+    ways = lax.axis_size(axis)
+    up = [(d, (d + 1) % ways) for d in range(ways)]
+    down = [(d, (d - 1) % ways) for d in range(ways)]
+    earlier, later = ([x], [x])
+    for _ in range(ways // 2):
+        earlier.append(lax.ppermute(earlier[-1], axis, up))
+    for _ in range((ways - 1) // 2):
+        later.append(lax.ppermute(later[-1], axis, down))
+    line = jnp.concatenate([*earlier[::-1], *later[1:]], axis=dim)
+    return jnp.roll(line, (lax.axis_index(axis) - ways // 2) * x.shape[dim], axis=dim)
+
+
 def split_bf16(values):
     high = values.astype(jnp.bfloat16)
     low = (values - high.astype(jnp.float32)).astype(jnp.bfloat16)
@@ -15,7 +28,7 @@
 
 
 def on_device(basis, potentials, orbitals, chan_orbital, pair_list, slot_list, coefs, exchange_ops):
-    all_orbitals = lax.all_gather(orbitals, "pcol", axis=0, tiled=True)
+    all_orbitals = collect(orbitals, "pcol", 0)
     row_devs = lax.axis_size("prow")
     col_devs = lax.axis_size("pcol")
     slot_count = row_devs * col_devs * CAP

time: 492 us -> 515 us (1.047)
  starting transfers between devices: 14.7 us -> 50.7 us
  blocking collectives: 18.1 us -> 0 us
  waiting for transfers between devices: 240 us -> 248 us
    ppermute x0 -> x15, starting transfers between devices: none -> 26.5 us  [the longest x7 24.8 us: collect(): later.append(lax.ppermute(later[-1], axis, down))]
    all_gather x1 -> x0, blocking collectives: 18.1 us -> none  [on_device(): all_orbitals = lax.all_gather(orbitals, 'pcol', axis=0, tiled=True)]
    all_to_all x1, starting transfers between devices: 14.7 us -> 24.2 us  [on_device(): received = lax.all_to_all(packed, ('prow', 'pcol'), 0, 0, tiled=True)]
    ppermute x0 -> x15, waiting for transfers between devices: none -> 7.38 us  [the longest x8 4.24 us: collect(): earlier.append(lax.ppermute(earlier[-1], axis, up))]
    unnamed x16 -> x23, local copies, waits for them, and re-layouts: 38.1 us -> 38.2 us
  transfers between devices with their start and end apart: 1 -> 16, of which waited for: 1 -> 10; matrix products, arithmetic and copies ran while one was open for 0% -> 13% of each run, Pallas kernels for 0% -> 0%
where the time goes in v1:
time: 515 us; the launch traced here: 513 us
  waiting for transfers between devices  248 us (48%)
  local copies, waits for them, and re-layouts  138 us (27%)
  matrix products  74.1 us (14%)
  starting transfers between devices  50.7 us (10%)
    all_to_all x1, waiting for transfers between devices, on_device(): received = lax.all_to_all(packed, ('prow', 'pcol'), 0, 0, tiled=True)  241 us
    concatenate x3, local copies, waits for them, and re-layouts, on_device(): jnp.concatenate([slot_exchange, slot_weight, slot_ids.astype(jnp.bfloat16...  49 us
    unnamed x23, local copies, waits for them, and re-layouts  38.2 us
    all_to_all x1, local copies, waits for them, and re-layouts, on_device(): received = lax.all_to_all(packed, ('prow', 'pcol'), 0, 0, tiled=True)  25.3 us
    dot_general x1, matrix products, on_device(): jnp.einsum('qa,gqb->gab', inner_rows, exchange_low, preferred_element_typ...  25 us
    ppermute x7, starting transfers between devices, collect(): later.append(lax.ppermute(later[-1], axis, down))  24.8 us
    all_to_all x1, starting transfers between devices, on_device(): received = lax.all_to_all(packed, ('prow', 'pcol'), 0, 0, tiled=True)  24.2 us
    dot_general x1, matrix products, on_device(): jnp.dot(matches.astype(jnp.bfloat16), exchange_rows, preferred_element_ty...  12.8 us
  transfers between devices with their start and end apart: 16, of which 10 were waited for; matrix products, arithmetic and copies ran while one was open for 13% of the time, Pallas kernels for 0%

profile of v1, /device:TPU:23, one launch (start us, length us, event | category | flops | bytes accessed | tf_op | source)
XLA Modules:
  0.0 512.9 jit_solution(13247662020091904132)
XLA Ops:
  0.0 0.0 copy-start
  0.0 1.6 collective-permute-start
  1.6 2.1 collective-permute-start.8
  3.7 13.9 %copy.29 = bf16[24,8,128,256]{3,1,2,0:T(8,128)(2,1)} copy(bf16[24,8,128,256]{3,2,1,0:T(8,128)(2,1)} %bitcast.29) | data formatting | bytes 25165824
  17.7 0.0 copy-done.4
  17.7 12.8 %convolution_convert_fusion = bf16[256,32768]{1,0:T(8,128)(2,1)} fusion(bf16[192,32768]{1,0:T(8,128)(2,1)} %bitcast.25, s32[192]{0:T(256)S(1)} %copy-done.4), kind=kOutput, calls=%fused_computation.2 | convolution fusion | flops 3229663232 | bytes 29360896 | tf_op jit(solution)/shard_map/dot_general | solution.py:74
  30.5 27.0 %concatenate.14 = bf16[128,2,32768]{2,1,0:T(2,128)(2,1)} reshape(bf16[256,32768]{1,0:T(8,128)(2,1)} %convolution_convert_fusion) | data formatting | bytes 33554432 | tf_op jit(solution)/shard_map/concatenate | solution.py:82
  57.4 0.0 collective-permute-done
  57.4 0.1 collective-permute-start.1
  57.5 14.1 %constant_dynamic-update-slice_fusion.1 = bf16[128,2,33408]{2,1,0:T(2,128)(2,1)} fusion(bf16[128,2,32768]{2,1,0:T(2,128)(2,1)} %concatenate.14), kind=kLoop, calls=%fused_computation.49 | loop fusion | bytes 33554432
  71.6 0.0 collective-permute-done.8
  71.6 3.6 collective-permute-start.9
  75.3 0.0 collective-permute-done.1
  75.3 0.0 collective-permute-start.2
  75.3 0.7 collective-permute-done.9
  76.0 3.8 collective-permute-start.10
  79.8 0.0 collective-permute-done.2
  79.8 0.0 collective-permute-start.3
  79.9 0.7 collective-permute-done.10
  80.6 3.8 collective-permute-start.11
  84.4 0.0 collective-permute-done.3
  84.4 0.0 collective-permute-start.4
  84.4 0.4 convolution_multiply_fusion.1
  84.8 0.4 collective-permute-done.11
  85.2 3.8 collective-permute-start.12
  89.0 0.0 collective-permute-done.4
  89.0 0.0 collective-permute-start.5
  89.0 0.7 collective-permute-done.12
  89.7 3.8 collective-permute-start.13
  93.5 0.1 collective-permute-done.5
  93.7 0.0 collective-permute-start.6
  93.7 0.2 select_reduce_fusion.2
  93.9 0.4 collective-permute-done.13
  94.3 3.8 collective-permute-start.14
  98.1 0.1 collective-permute-done.6
  98.2 0.0 collective-permute-start.7
  98.2 0.1 select_reduce_fusion
  98.4 0.2 convert_element_type.87
  98.7 0.2 collective-permute-done.14
  98.9 4.0 collective-permute-done.7
  102.8 0.0 copy-done.5
  102.8 0.5 concatenate.15
  103.3 0.2 fusion.19
  103.5 0.3 fusion.14
  103.8 0.5 convolution_convert_fusion.1
  104.3 0.1 concatenate.16
  104.4 0.9 constant_dynamic-update-slice_fusion
  105.3 3.3 dynamic-update-slice.2
  108.6 21.9 %dynamic-update-slice.3 = bf16[128,2,33408]{2,1,0:T(2,128)(2,1)} dynamic-update-slice(bf16[128,2,33408]{2,1,0:T(2,128)(2,1)} %dynamic-update-slice.2, bf16[128,2,127]{2,1,0:T(2,128)(2,1)S(1)} %broadcast_in_dim.52, s32[]{} %constant.88, s32[]{} %constant.88, s32[]{} %constant.91) | dynamic-update-slice | bytes 130052 | tf_op jit(solution)/shard_map/concatenate | solution.py:82
  130.6 0.0 copy-start.3
  130.6 24.2 %all-to-all-start = ((bf16[128,2,33408]{2,1,0:T(2,128)(2,1)}), bf16[128,2,33408]{2,1,0:T(2,128)(2,1)}, u32[]{:S(2)}, u32[]{:S(2)}) async-start(bf16[128,2,33408]{2,1,0:T(2,128)(2,1)} %dynamic-update-slice.3), calls=%async_computation | async-start | bytes 34209792 | tf_op jit(solution)/shard_map/all_to_all | solution.py:91
  154.8 0.1 copy.25
  155.0 241.0 %all-to-all-done = bf16[128,2,33408]{2,1,0:T(2,128)(2,1)} async-done(((bf16[128,2,33408]{2,1,0:T(2,128)(2,1)}), bf16[128,2,33408]{2,1,0:T(2,128)(2,1)}, u32[]{:S(2)}, u32[]{:S(2)}) %all-to-all-start) | async-done | bytes 17104928 | tf_op jit(solution)/shard_map/all_to_all | solution.py:91
  395.9 25.3 %all_to_all.7 = bf16[256,33408]{1,0:T(8,128)(2,1)} reshape(bf16[128,2,33408]{2,1,0:T(2,128)(2,1)} %all-to-all-done) | data formatting | bytes 34209792 | tf_op jit(solution)/shard_map/all_to_all | solution.py:91
  421.2 1.0 convert_reduce_fusion
  422.1 7.5 %fusion.2 = f32[64,33280]{1,0:T(8,128)S(1)} fusion(bf16[256,33408]{1,0:T(8,128)(2,1)} %all_to_all.7, s32[256]{0:T(256)S(1)} %convert_reduce_fusion), kind=kOutput, calls=%fused_computation.5 | convolution fusion | flops 1090535424 | bytes 25560064 | tf_op jit(solution)/shard_map/dot_general | solution.py:96
  429.6 3.9 slice.43
  433.6 8.1 %fusion.4 = f32[64,256,256]{2,1,0:T(8,128)} fusion(f32[512,256]{0,1:T(8,128)S(1)} %copy.25, f32[64,512]{1,0:T(8,128)S(1)} %slice.42, bf16[512,256]{1,0:T(8,128)(2,1)S(1)} %copy-done.3), kind=kOutput, calls=%fused_computation.7 | convolution fusion | flops 4336910336 | bytes 17694720 | tf_op jit(solution)/shard_map/qa,gqb->gab/dot_general | solution.py:107
  441.6 8.0 %fusion.1 = f32[64,256,256]{2,1,0:T(8,128)} fusion(f32[512,256]{0,1:T(8,128)S(1)} %copy.25, f32[64,512]{1,0:T(8,128)S(1)} %slice.42, bf16[512,256]{1,0:T(8,128)(2,1)S(1)} %copy-done.3), kind=kOutput, calls=%fused_computation.4 | convolution fusion | flops 4311744512 | bytes 17694720 | tf_op jit(solution)/shard_map/qa,gqb->gab/dot_general | solution.py:106
  449.7 5.9 %copy.30 = f32[8,8,128,256]{3,2,1,0:T(8,128)} copy(f32[8,8,128,256]{3,1,2,0:T(8,128)S(1)} %bitcast.27) | data formatting | bytes 16777216
  455.6 9.0 %copy.26 = f32[64,128,256]{1,2,0:T(8,128)} copy(f32[64,128,256]{2,1,0:T(8,128)} %bitcast.28) | data formatting | bytes 16777216 | tf_op jit(solution)/shard_map/reshape | solution.py:97
  464.6 11.5 %fusion.11 = f32[64,256,256]{2,1,0:T(8,128)} fusion(f32[64,128,256]{1,2,0:T(8,128)} %copy.26, bf16[512,256]{1,0:T(8,128)(2,1)S(1)} %copy-done.3), kind=kOutput, calls=%fused_computation.15 | convolution fusion | flops 1075838976 | bytes 25231360 | tf_op jit(solution)/shard_map/qa,gqb->gab/dot_general | solution.py:108
  476.0 25.0 %add_convert_fusion = bf16[64,256,256]{2,1,0:T(8,128)(2,1)} fusion(f32[64,256,256]{2,1,0:T(8,128)} %fusion.11, f32[64,256,256]{2,1,0:T(8,128)} %fusion.1, f32[64,256,256]{2,1,0:T(8,128)} %fusion.4, f32[64,128,256]{1,2,0:T(8,128)} %copy.26, bf16[512,256]{1,0:T(8,128)(2,1)S(1)} %copy-done.3), kind=kOutput, calls=%fused_computation.8 | convolution fusion | flops 1098907648 | bytes 67174400 | tf_op jit(solution)/shard_map/qa,gqb->gab/dot_general | solution.py:109
  501.0 11.9 %copy.28 = bf16[32,1,2,1,256,256]{5,4,3,2,1,0:T(8,128)(2,1)} copy(bf16[32,1,2,1,256,256]{4,5,2,0,3,1:T(8,128)(2,1)} %bitcast.26) | data formatting | bytes 16777216 | tf_op jit(solution)/shard_map/reshape | solution.py:111
  (20 shorter events, 0.1 us)
Async XLA Ops:
  0.0 84.4 %copy-start = (f32[8,512]{1,0:T(8,128)S(1)}, f32[8,512]{1,0:T(8,128)}, u32[]{:S(2)}) copy-start(f32[8,512]{1,0:T(8,128)} %param.9) | copy-start | bytes 49156
  0.0 17.7 %copy-start.4 = (s32[192]{0:T(256)S(1)}, s32[192]{0:T(256)}, u32[]{:S(2)}) copy-start(s32[192]{0:T(256)} %param.13) | copy-start | bytes 2308
  0.0 57.4 %collective-permute-start = (bf16[4,512]{1,0:T(4,128)(2,1)}, bf16[4,512]{1,0:T(4,128)(2,1)S(1)}, u32[]{:S(2)}, u32[]{:S(2)}) collective-permute-start(bf16[4,512]{1,0:T(4,128)(2,1)} %param.10), channel_id=1, source_target_pairs={{0,1},{1,2},{2,3},{3,4},{4,5},{5,6},{6,7},{7,8},{8,9},{9,10},{10,1... | collective-permute-start | bytes 12296 | tf_op jit(solution)/shard_map/ppermute | solution.py:17
  1.6 70.0 %collective-permute-start.8 = (bf16[4,512]{1,0:T(4,128)(2,1)}, bf16[4,512]{1,0:T(4,128)(2,1)S(1)}, u32[]{:S(2)}, u32[]{:S(2)}) collective-permute-start(bf16[4,512]{1,0:T(4,128)(2,1)} %param.10), channel_id=1, source_target_pairs={{0,15},{1,0},{2,1},{3,2},{4,3},{5,4},{6,5},{7,6},{8,7},{9,8},{10,9... | collective-permute-start | bytes 12296 | tf_op jit(solution)/shard_map/ppermute | solution.py:19
  57.4 17.9 %copy-start.6 = (s32[192,3]{0,1:T(4,128)S(1)}, s32[192,3]{0,1:T(4,128)}, u32[]{:S(2)}) copy-start(s32[192,3]{0,1:T(4,128)} %param.12) | copy-start | bytes 6916
  57.4 22.4 %copy-start.7 = (f32[192,2]{0,1:T(2,128)S(1)}, f32[192,2]{0,1:T(2,128)}, u32[]{:S(2)}) copy-start(f32[192,2]{0,1:T(2,128)} %param.14) | copy-start | bytes 4612
  57.4 36.3 %copy-start.8 = (s32[256]{0:T(256)S(1)}, s32[256]{0:T(256)}, u32[]{:S(2)}) copy-start(s32[256]{0:T(256)} %param.11) | copy-start | bytes 3076
  57.4 45.4 %copy-start.5 = (bf16[4,512]{1,0:T(4,128)(2,1)S(1)}, bf16[4,512]{1,0:T(4,128)(2,1)}, u32[]{:S(2)}) copy-start(bf16[4,512]{1,0:T(4,128)(2,1)} %param.10) | copy-start | bytes 12292
  57.4 17.8 %collective-permute-start.1 = (bf16[4,512]{1,0:T(4,128)(2,1)S(1)}, bf16[4,512]{1,0:T(4,128)(2,1)S(1)}, u32[]{:S(2)}, u32[]{:S(2)}) collective-permute-start(bf16[4,512]{1,0:T(4,128)(2,1)S(1)} %collective-permute-done), channel_id=1, source_target_pairs={{0,1},{1,2},{2,3},{3,4},{4,5},{5,6},{6,7},{7,8},{8,9},{9,10},{10,1... | collective-permute-start | bytes 12296 | tf_op jit(solution)/shard_map/ppermute | solution.py:17
  71.6 4.4 collective-permute-start.9
  75.3 4.6 collective-permute-start.2
  76.0 4.6 collective-permute-start.10
  79.8 4.6 collective-permute-start.3
  80.6 4.6 collective-permute-start.11
  84.4 4.6 collective-permute-start.4
  85.2 4.6 collective-permute-start.12
  89.0 4.7 collective-permute-start.5
  89.7 4.6 collective-permute-start.13
  93.7 4.6 collective-permute-start.6
  94.3 4.6 collective-permute-start.14
  98.2 4.6 collective-permute-start.7
  130.6 24.2 %copy-start.3 = (bf16[512,256]{1,0:T(8,128)(2,1)S(1)}, bf16[512,256]{1,0:T(8,128)(2,1)}, u32[]{:S(2)}) copy-start(bf16[512,256]{1,0:T(8,128)(2,1)} %param.8) | copy-start | bytes 786436
  130.6 265.4 %all-to-all-start = ((bf16[128,2,33408]{2,1,0:T(2,128)(2,1)}), bf16[128,2,33408]{2,1,0:T(2,128)(2,1)}, u32[]{:S(2)}, u32[]{:S(2)}) async-start(bf16[128,2,33408]{2,1,0:T(2,128)(2,1)} %dynamic-update-slice.3), calls=%async_computation | async-start | bytes 34209792 | tf_op jit(solution)/shard_map/all_to_all | solution.py:91
  441.6 8.0 %copy-start.2 = (f32[64,32768]{1,0:T(8,128)S(1)}, f32[64,32768]{1,0:T(8,128)}, u32[]{:S(2)}) copy-start(f32[64,32768]{1,0:T(8,128)} %slice.43) | copy-start | bytes 25165828
  476.0 36.9 %copy-start.1 = (f32[8,512]{1,0:T(8,128)S(1)}, f32[8,512]{1,0:T(8,128)}, u32[]{:S(2)}) copy-start(f32[8,512]{1,0:T(8,128)} %param.9) | copy-start | bytes 49156
